TPU v7x, 32 devices: a whole 2x2x4 slice. The times are simulated.
32 devices in a mesh: groups: 2 (over y), ctx: 4 (over z), head: 4 (over x, core).
Axes of the slice: x: 2, y: 2, z: 4, core: 2. Of those that a mesh axis runs over, the one named last changes fastest.
Arguments:
- queries: bfloat16 [8192, 512], P(('groups', 'ctx', 'head')), parts along dimension 0, may hold values from -8 to 8, as said below
- keys: bfloat16 [8192, 512], P(('groups', 'ctx', 'head')), parts along dimension 0, may hold values from -8 to 8
- values: bfloat16 [8192, 4096], P(('groups', 'ctx', 'head')), parts along dimension 0, may hold values from -6 to 6
- gain: float32 [4096], P('head'), may hold values from 0.5 to 1.5
Outputs:
- mixed: bfloat16 [8192, 4096], P(('groups', 'ctx', 'head')), parts along dimension 0
There are 2 independent parts, one for each index of `groups`. A program takes and returns all parts, laid end to end along the dimension named above; an argument that names none is the same for every part. Nothing has to cross between parts.
Inputs may be any that keep to these rules, and one draw needn't show every extreme that they name: `queries`: query entries lie in the stated range.
All inputs are finite; a program needn't handle non-finite values.
Results may differ from a plain program's by a relative error of at most 0.0054.
Values may be sent and summed in bfloat16 or wider, within the bound.
No kernel may reach another device: no remote copies, remote signals or barrier semaphores. Data moves between devices by JAX's collectives and lax.ppermute only.
A program may use at most 128 MiB of HBM per device.

v0:
```python
import math
import jax
import jax.numpy as jnp
from jax import lax
from jax.sharding import PartitionSpec as P

HEADS = 32
KD = 16
VD = 128
WINDOW = 64
outer_scale = 1.0 / (4.0 * math.sqrt(2.0))
epsilon = 1e-06


def shifted(shard, axis, by):
    peers = lax.axis_size(axis)
    pairs = [(i, i + by) for i in range(peers) if 0 <= i + by < peers]
    return lax.ppermute(shard, axis, pairs)


def entering(shard, axis, combine, identity):
    peers, here = (lax.axis_size(axis), lax.axis_index(axis))
    everything = lax.all_gather(shard, axis)
    start = jnp.broadcast_to(jnp.asarray(identity, shard.dtype), shard.shape)

    def hop(k, before):
        reached = k < here
        new = combine(before, everything[k])
        return jnp.where(reached, new, before)

    return lax.fori_loop(0, peers, hop, start)


def feature_map(vector):
    width = vector.shape[-1]
    products = (vector[..., :, None] * vector[..., None, :]).reshape(
        vector.shape[:-1] + (width * width,)
    )
    unit_column = jnp.ones(vector.shape[:-1] + (1,), jnp.float32)
    return jnp.concatenate([unit_column, vector * 0.5, products * outer_scale], axis=-1)


def per_device(queries, keys, values, gain):
    local_tokens = queries.shape[0]
    query_tok = queries.reshape(local_tokens, HEADS, KD)
    key_tok = keys.reshape(local_tokens, HEADS, KD)
    value_tok = values.reshape(local_tokens, HEADS, VD)
    query_head, key_head, value_head = (
        lax.all_to_all(query_tok, "head", split_axis=1, concat_axis=0, tiled=True),
        lax.all_to_all(key_tok, "head", split_axis=1, concat_axis=0, tiled=True),
        lax.all_to_all(value_tok, "head", split_axis=1, concat_axis=0, tiled=True),
    )
    span_rows = query_head.shape[0]
    heads_here = query_head.shape[1]
    block_rows = min(512, span_rows)
    block_count = span_rows // block_rows
    tail_keys, tail_values = shifted(
        (key_head[span_rows - WINDOW :], value_head[span_rows - WINDOW :]), "ctx", 1
    )
    key_ext = jnp.concatenate([tail_keys, key_head], axis=0)
    value_ext = jnp.concatenate([tail_values, value_head], axis=0)
    first_span = lax.axis_index("ctx") == 0
    key_features = feature_map(key_head.astype(jnp.float32)).astype(jnp.bfloat16)
    own_state = jnp.einsum(
        "bhf,bhv->hfv", key_features, value_head, preferred_element_type=jnp.float32
    )

    def combine_states(earlier, later):
        return earlier + later

    prefix = entering(own_state, "ctx", combine_states, jnp.zeros_like(own_state))

    def block_step(state, block_index):
        start = block_index * block_rows
        query_block = lax.dynamic_slice_in_dim(query_head, start, block_rows, 0)
        key_block = lax.dynamic_slice_in_dim(key_head, start, block_rows, 0)
        value_block = lax.dynamic_slice_in_dim(value_head, start, block_rows, 0)
        key_feat = lax.dynamic_slice_in_dim(key_features, start, block_rows, 0)
        key_window = lax.dynamic_slice_in_dim(key_ext, start, block_rows + WINDOW, 0)
        value_window = lax.dynamic_slice_in_dim(value_ext, start, block_rows + WINDOW, 0)
        scores = (
            jnp.einsum("bhd,chd->hbc", query_block, key_block, preferred_element_type=jnp.float32)
            * 0.25
        )
        row_pos = jnp.arange(block_rows)[:, None]
        col_pos = jnp.arange(block_rows)[None, :]
        kernel = jnp.where(col_pos <= row_pos, 1.0 + scores + 0.5 * scores * scores, 0.0).astype(
            jnp.bfloat16
        )
        intra = jnp.einsum("hbc,chv->bhv", kernel, value_block, preferred_element_type=jnp.float32)
        query_feat = feature_map(query_block.astype(jnp.float32)).astype(jnp.bfloat16)
        inter = jnp.einsum(
            "bhf,hfv->bhv",
            query_feat,
            state.astype(jnp.bfloat16),
            preferred_element_type=jnp.float32,
        )
        state = state + jnp.einsum(
            "bhf,bhv->hfv", key_feat, value_block, preferred_element_type=jnp.float32
        )
        window_scores = (
            jnp.einsum("bhd,chd->hbc", query_block, key_window, preferred_element_type=jnp.float32)
            * 0.25
        )
        key_pos = jnp.arange(block_rows + WINDOW)[None, :] - WINDOW
        valid = (
            (key_pos <= row_pos)
            & (key_pos > row_pos - WINDOW)
            & ((start + key_pos >= 0) | jnp.logical_not(first_span))
        )
        masked = jnp.where(valid, window_scores, -jnp.inf)
        highest_score = jnp.max(masked, axis=2, keepdims=True)
        expo = jnp.where(valid, jnp.exp(window_scores - highest_score), 0.0)
        weights = (expo / jnp.sum(expo, axis=2, keepdims=True)).astype(jnp.bfloat16)
        window_out = jnp.einsum(
            "hbc,chv->bhv", weights, value_window, preferred_element_type=jnp.float32
        )
        return (state, (intra + inter, window_out))

    final_state, (linear_all, window_all) = lax.scan(block_step, prefix, jnp.arange(block_count))
    linear = linear_all.reshape(span_rows, heads_here, VD)
    window = window_all.reshape(span_rows, heads_here, VD)
    scale = lax.rsqrt(jnp.mean(linear * linear, axis=2, keepdims=True) + epsilon)
    gains = gain.reshape(heads_here, VD)
    mixed = (linear * scale * gains + window).astype(jnp.bfloat16)
    tokens_back = lax.all_to_all(mixed, "head", split_axis=0, concat_axis=1, tiled=True)
    return tokens_back.reshape(tokens_back.shape[0], HEADS * VD)


def solution(mesh):
    placed = (
        P(("groups", "ctx", "head"), None),
        P(("groups", "ctx", "head"), None),
        P(("groups", "ctx", "head"), None),
        P("head"),
    )
    return jax.shard_map(
        per_device,
        mesh=mesh,
        in_specs=placed,
        out_specs=P(("groups", "ctx", "head"), None),
        check_vma=False,
    )
```

profile of v0, /device:TPU:0, one launch (start us, length us, event | category | flops | bytes accessed | tf_op | source)
XLA Modules:
  0.0 278.9 jit_solution(16457745592861958230)
XLA Ops:
  6.5 1.8 copy.42
  8.3 4.2 %all-to-all-start = ((bf16[256,32,16]{0,2,1:T(8,128)(2,1)}), bf16[256,32,16]{0,2,1:T(8,128)(2,1)S(1)}, u32[]{:S(2)}, u32[]{:S(2)}) async-start(bf16[256,32,16]{0,2,1:T(8,128)(2,1)} %bitcast.7), calls=%async_computation | async-start | bytes 524288 | tf_op jit(solution)/shard_map/all_to_all | solution.py:50
  12.5 3.3 %copy.44 = bf16[256,4096]{0,1:T(8,128)(2,1)S(1)} copy(bf16[256,4096]{1,0:T(8,128)(2,1)} %param.10) | data formatting | bytes 4194304 | tf_op args[2]
  15.8 2.9 %copy.45 = bf16[256,32,128]{2,0,1:T(8,128)(2,1)} copy(bf16[256,32,128]{0,2,1:T(8,128)(2,1)S(1)} %bitcast.80) | data formatting | bytes 4194304 | tf_op jit(solution)/shard_map/reshape | solution.py:47
  18.7 3.6 %all-to-all-start.1 = ((bf16[256,32,128]{2,0,1:T(8,128)(2,1)}), bf16[256,32,128]{2,0,1:T(8,128)(2,1)S(1)}, u32[]{:S(2)}, u32[]{:S(2)}) async-start(bf16[256,32,128]{2,0,1:T(8,128)(2,1)} %copy.45), calls=%async_computation.1 | async-start | bytes 4194304 | tf_op jit(solution)/shard_map/all_to_all | solution.py:51
  22.5 1.3 multiply_convert_fusion.2
  23.8 3.9 %pad_maximum_fusion = bf16[1024,8,273]{0,2,1:T(8,128)(2,1)} fusion(bf16[1024,8,256]{0,2,1:T(8,128)(2,1)S(1)} %bitcast.76, bf16[1024,8,16]{0,2,1:T(8,128)(2,1)S(1)} %multiply_convert_fusion.3, bf16[273]{0:T(512)(128)(2,1)S(1)} %pad.7.clone), kind=kLoop, calls=%fused_computation.66 | loop fusion | flops 13418496 | bytes 8929826 | tf_op jit(solution)/shard_map/concatenate | solution.py:40
  27.7 20.3 %all-to-all-done.1 = bf16[256,32,128]{2,0,1:T(8,128)(2,1)S(1)} async-done(((bf16[256,32,128]{2,0,1:T(8,128)(2,1)}), bf16[256,32,128]{2,0,1:T(8,128)(2,1)S(1)}, u32[]{:S(2)}, u32[]{:S(2)}) %all-to-all-start.1) | async-done | bytes 2097184 | tf_op jit(solution)/shard_map/all_to_all | solution.py:51
  48.0 1.5 copy.47
  49.4 4.4 %fusion.77 = f32[8,273,128]{2,1,0:T(8,128)S(1)} fusion(bf16[1024,8,273]{0,2,1:T(8,128)(2,1)} %pad_maximum_fusion, bf16[1024,8,128]{2,0,1:T(8,128)(2,1)} %bitcast.15), kind=kOutput, calls=%fused_computation.77 | convolution fusion | flops 572522496 | bytes 7688192 | tf_op jit(solution)/shard_map/bhf,bhv->hfv/dot_general | solution.py:64
  53.8 1.3 copy.48
  55.1 0.8 copy.50
  55.9 3.4 %all-to-all-start.2 = ((bf16[256,32,16]{0,2,1:T(8,128)(2,1)}), bf16[256,32,16]{0,2,1:T(8,128)(2,1)S(1)}, u32[]{:S(2)}, u32[]{:S(2)}) async-start(bf16[256,32,16]{0,2,1:T(8,128)(2,1)} %bitcast.17), calls=%async_computation.2 | async-start | bytes 524288 | tf_op jit(solution)/shard_map/all_to_all | solution.py:49
  59.4 4.1 %collective-permute-start.1 = (bf16[64,8,16]{0,2,1:T(8,128)(2,1)S(1)}, bf16[64,8,16]{0,2,1:T(8,128)(2,1)S(1)}, u32[]{:S(2)}, u32[]{:S(2)}) collective-permute-start(bf16[64,8,16]{0,2,1:T(8,128)(2,1)S(1)} %slice.9), channel_id=1, source_target_pairs={{0,4},{4,8},{8,12},{1,5},{5,9},{9,13},{2,6},{6,10},{10,14},{3,7},{... | collective-permute-start | bytes 49160 | tf_op jit(solution)/shard_map/ppermute | solution.py:18
  63.6 1.7 all-to-all-done.2
  65.3 0.8 copy.65
  66.1 0.9 slice.8
  67.0 4.3 %collective-permute-start = (bf16[64,8,128]{2,0,1:T(8,128)(2,1)S(1)}, bf16[64,8,128]{2,0,1:T(8,128)(2,1)S(1)}, u32[]{:S(2)}, u32[]{:S(2)}) collective-permute-start(bf16[64,8,128]{2,0,1:T(8,128)(2,1)S(1)} %slice.8), channel_id=1, source_target_pairs={{0,4},{4,8},{8,12},{1,5},{5,9},{9,13},{2,6},{6,10},{10,14},{3,7},{... | collective-permute-start | bytes 393224 | tf_op jit(solution)/shard_map/ppermute | solution.py:18
  71.4 0.9 pad_maximum_fusion.2
  72.2 5.1 %collective-permute-done = bf16[64,8,128]{2,0,1:T(8,128)(2,1)S(1)} collective-permute-done((bf16[64,8,128]{2,0,1:T(8,128)(2,1)S(1)}, bf16[64,8,128]{2,0,1:T(8,128)(2,1)S(1)}, u32[]{:S(2)}, u32[]{:S(2)}) %collective-permute-start) | collective-permute-done | bytes 131104 | tf_op jit(solution)/shard_map/ppermute | solution.py:18
  77.4 3.1 %pad_maximum_fusion.1 = bf16[1088,8,128]{2,0,1:T(8,128)(2,1)} fusion(bf16[1024,8,128]{2,0,1:T(8,128)(2,1)} %bitcast.15, bf16[64,8,128]{2,0,1:T(8,128)(2,1)S(1)} %collective-permute-done), kind=kLoop, calls=%fused_computation.72 | loop fusion | flops 4456448 | bytes 4456448 | tf_op jit(solution)/shard_map/concatenate | solution.py:61
  80.5 65.2 %all-gather.3.cloned.1.call-done = f32[32,273,128]{2,0,1:T(8,128)} async-done(((f32[8,273,128]{2,0,1:T(8,128)}), f32[32,273,128]{2,0,1:T(8,128)}) %all-gather.3.cloned.1.call-update) | async-done | bytes 4472848 | tf_op jit(solution)/shard_map/all_gather | solution.py:23
  145.7 7.5 %while.32 = (s32[]{:T(128)}, f32[8,273,128]{2,1,0:T(8,128)S(1)}, s32[]{:T(128)}, f32[4,8,273,128]{3,1,0,2:T(8,128)}, s32[]{:T(128)}, /*index=5*/s32[]{:T(128)}) while((s32[]{:T(128)}, f32[8,273,128]{2,1,0:T(8,128)S(1)}, s32[]{:T(128)}, f32[4,8,273,128]{3,1,0,2:T(8,128)}, s32[]{:T(128)}, /*index=5*/s32[]{:T(128)}) %tuple.69), condition=%wide.region_1.2_spmd.clone, body=%wide.region_0.1_spmd.clone.sunk | while | flops 838660 | bytes 5591141 | solution.py:31
  145.7 1.3 constant_dynamic-slice_fusion.2
  147.0 0.5 add_select_fusion.2
  147.6 1.3 constant_dynamic-slice_fusion.2
  148.9 0.5 add_select_fusion.2
  149.5 1.3 constant_dynamic-slice_fusion.2
  150.8 0.5 add_select_fusion.2
  151.4 1.3 constant_dynamic-slice_fusion.2
  152.7 0.5 add_select_fusion.2
  153.2 71.0 %while.31 = (s32[]{:T(128)}, f32[8,273,128]{2,1,0:T(8,128)S(1)}, f32[2,512,8,128]{1,3,2,0:T(8,128)}, f32[2,512,8,128]{3,2,1,0:T(8,128)}, s32[2]{0:T(128)S(1)}, /...) while((s32[]{:T(128)}, f32[8,273,128]{2,1,0:T(8,128)S(1)}, ...), condition=%wide.region_5.6_spmd, body=%wide.region_2.5_spmd.sunk | while | flops 1977677568 | bytes 70311560 | solution.py:120
  153.3 0.6 dynamic_slice.126
  154.5 1.6 multiply_convert_fusion.7
  156.1 0.9 dynamic-slice_convert_fusion.2
  157.0 0.8 iota_compare_fusion.3
  157.9 1.1 fusion.113
  158.9 4.5 %fusion.111 = f32[8,128,512]{2,1,0:T(8,128)S(1)} fusion(pred[512,512]{1,0:T(8,128)(4,1)} %iota_compare_fusion.3, bf16[1024,8,128]{2,0,1:T(8,128)(2,1)} %get-tuple-element.495, s32[]{:T(128)S(6)} %select_n.84, bf16[1024,8,16]{0,2,1:T(8,128)(2,1)} %copy-done.1, bf16[1024,8,16]{0,2,1:T(8,128)(2,1)} %get-tuple-element.496), kind=kOutput, calls=%fused_computation.12.clone.1 | convolution fusion | flops 618659840 | bytes 3671552 | tf_op jit(solution)/shard_map/while/body/eval_jaxpr/hbc,chv->bhv/dot_general | solution.py:90
  163.5 0.7 multiply_convert_fusion.6
  164.2 3.7 %bitcast_dynamic-update-slice_fusion.2 = f32[2,512,8,128]{1,3,2,0:T(8,128)} fusion(f32[2,512,8,128]{1,3,2,0:T(8,128)} %get-tuple-element.472, s32[]{:T(128)S(6)} %copy.85, f32[8,128,512]{2,1,0:T(8,128)S(1)} %fusion.111, bf16[512,8,256]{0,2,1:T(8,128)(2,1)S(1)} %bitcast.73, bf16[512,8,16]{0,2,1:T(8,128)(2,1)} %multiply_convert_fusion.7, ...), kind=kOutput, calls=%fused_computation.22.clone.1 | convolution fusion | flops 293774336 | bytes 7541286 | tf_op jit(solution)/shard_map/while/body/eval_jaxpr/bhf,hfv->bhv/dot_general | solution.py:92
  167.9 2.3 fusion.110
  170.2 8.4 %fusion.114 = (f32[8,512]{1,0:T(8,128)S(1)}, f32[8,512,576]{1,2,0:T(8,128)}) fusion(pred[512,576]{0,1:T(8,128)(4,1)S(1)} %copy-done, bf16[1088,8,16]{0,2,1:T(8,128)(2,1)S(1)} %copy-done.3, s32[]{:T(128)S(6)} %select_n.85, bf16[1024,8,16]{0,2,1:T(8,128)(2,1)} %get-tuple-element.496, s32[]{:T(128)S(6)} %select_n.84), kind=kOutput, calls=%fused_computation.76.clone.1 | convolution fusion | flops 165151296 | bytes 10635264 | tf_op jit(solution)/shard_map/while/body/eval_jaxpr/sub | solution.py:113
  178.6 6.5 %fusion.115 = f32[1,512,8,128]{1,3,2,0:T(8,128)} fusion(f32[8,512,576]{1,2,0:T(8,128)} %get-tuple-element.427, f32[8,512]{1,0:T(8,128)S(1)} %get-tuple-element.428, bf16[1088,8,128]{2,0,1:T(8,128)(2,1)} %get-tuple-element.498, s32[]{:T(128)S(6)} %select_n.85), kind=kOutput, calls=%fused_computation.24.clone.1 | convolution fusion | flops 608698368 | bytes 12730372 | tf_op jit(solution)/shard_map/while/body/eval_jaxpr/hbc,chv->bhv/dot_general | solution.py:115
  185.1 2.1 copy.71
  187.2 1.5 constant_dynamic-update-slice_fusion.2
  188.7 0.7 dynamic_slice.126
  190.0 1.6 multiply_convert_fusion.7
  191.6 0.9 dynamic-slice_convert_fusion.2
  192.5 0.8 iota_compare_fusion.3
  193.3 1.1 fusion.113
  194.4 4.6 %fusion.111 = f32[8,128,512]{2,1,0:T(8,128)S(1)} fusion(pred[512,512]{1,0:T(8,128)(4,1)} %iota_compare_fusion.3, bf16[1024,8,128]{2,0,1:T(8,128)(2,1)} %get-tuple-element.495, s32[]{:T(128)S(6)} %select_n.84, bf16[1024,8,16]{0,2,1:T(8,128)(2,1)} %copy-done.1, bf16[1024,8,16]{0,2,1:T(8,128)(2,1)} %get-tuple-element.496), kind=kOutput, calls=%fused_computation.12.clone.1 | convolution fusion | flops 618659840 | bytes 3671552 | tf_op jit(solution)/shard_map/while/body/eval_jaxpr/hbc,chv->bhv/dot_general | solution.py:90
  199.0 0.7 multiply_convert_fusion.6
  199.6 3.7 %bitcast_dynamic-update-slice_fusion.2 = f32[2,512,8,128]{1,3,2,0:T(8,128)} fusion(f32[2,512,8,128]{1,3,2,0:T(8,128)} %get-tuple-element.472, s32[]{:T(128)S(6)} %copy.85, f32[8,128,512]{2,1,0:T(8,128)S(1)} %fusion.111, bf16[512,8,256]{0,2,1:T(8,128)(2,1)S(1)} %bitcast.73, bf16[512,8,16]{0,2,1:T(8,128)(2,1)} %multiply_convert_fusion.7, ...), kind=kOutput, calls=%fused_computation.22.clone.1 | convolution fusion | flops 293774336 | bytes 7541286 | tf_op jit(solution)/shard_map/while/body/eval_jaxpr/bhf,hfv->bhv/dot_general | solution.py:92
  203.4 2.3 fusion.110
  205.7 8.4 %fusion.114 = (f32[8,512]{1,0:T(8,128)S(1)}, f32[8,512,576]{1,2,0:T(8,128)}) fusion(pred[512,576]{0,1:T(8,128)(4,1)S(1)} %copy-done, bf16[1088,8,16]{0,2,1:T(8,128)(2,1)S(1)} %copy-done.3, s32[]{:T(128)S(6)} %select_n.85, bf16[1024,8,16]{0,2,1:T(8,128)(2,1)} %get-tuple-element.496, s32[]{:T(128)S(6)} %select_n.84), kind=kOutput, calls=%fused_computation.76.clone.1 | convolution fusion | flops 165151296 | bytes 10635264 | tf_op jit(solution)/shard_map/while/body/eval_jaxpr/sub | solution.py:113
  214.1 6.5 %fusion.115 = f32[1,512,8,128]{1,3,2,0:T(8,128)} fusion(f32[8,512,576]{1,2,0:T(8,128)} %get-tuple-element.427, f32[8,512]{1,0:T(8,128)S(1)} %get-tuple-element.428, bf16[1088,8,128]{2,0,1:T(8,128)(2,1)} %get-tuple-element.498, s32[]{:T(128)S(6)} %select_n.85), kind=kOutput, calls=%fused_computation.24.clone.1 | convolution fusion | flops 608698368 | bytes 12730372 | tf_op jit(solution)/shard_map/while/body/eval_jaxpr/hbc,chv->bhv/dot_general | solution.py:115
  220.6 2.1 copy.71
  222.7 1.5 constant_dynamic-update-slice_fusion.2
  224.2 2.8 multiply_reduce_fusion
  227.0 5.3 %copy.52 = f32[2,512,8,128]{3,2,1,0:T(8,128)} copy(f32[2,512,8,128]{1,3,2,0:T(8,128)} %get-tuple-element.272) | data formatting | bytes 8388608 | tf_op jit(solution)/shard_map/while | solution.py:120
  232.5 4.1 %fusion.66 = bf16[1024,8,128]{2,1,0:T(8,128)(2,1)S(1)} fusion(f32[2,512,8,128]{3,2,1,0:T(8,128)} %get-tuple-element.273, f32[2,512,8,128]{3,2,1,0:T(8,128)} %copy.52, f32[8,128]{1,0:T(8,128)S(1)} %bitcast.90, f32[1024,8]{1,0:T(8,128)S(1)} %copy.53), kind=kLoop, calls=%fused_computation.68 | loop fusion | flops 4194304 | bytes 10522624 | tf_op jit(solution)/shard_map/convert_element_type | solution.py:125
  236.6 28.8 %all_to_all.69 = bf16[1024,8,128]{2,1,0:T(8,128)(2,1)S(1)} all-to-all(bf16[1024,8,128]{2,1,0:T(8,128)(2,1)S(1)} %fusion.66), channel_id=1, replica_groups=mesh['groups'=2,'ctx'=4,'head'=4] {'head'}, dimensions={0} | all-to-all | bytes 4194304 | tf_op jit(solution)/shard_map/all_to_all | solution.py:126
  265.4 2.6 copy.55
  268.0 4.1 %copy.56 = bf16[256,4096]{1,0:T(8,128)(2,1)} copy(bf16[256,4096]{0,1:T(8,128)(2,1)} %bitcast.79) | data formatting | bytes 4194304 | tf_op jit(solution)/shard_map/reshape | solution.py:127
  (53 shorter events, 0.6 us)
Async XLA Ops:
  8.3 10.3 %all-to-all-start = ((bf16[256,32,16]{0,2,1:T(8,128)(2,1)}), bf16[256,32,16]{0,2,1:T(8,128)(2,1)S(1)}, u32[]{:S(2)}, u32[]{:S(2)}) async-start(bf16[256,32,16]{0,2,1:T(8,128)(2,1)} %bitcast.7), calls=%async_computation | async-start | bytes 524288 | tf_op jit(solution)/shard_map/all_to_all | solution.py:50
  18.7 29.3 %all-to-all-start.1 = ((bf16[256,32,128]{2,0,1:T(8,128)(2,1)}), bf16[256,32,128]{2,0,1:T(8,128)(2,1)S(1)}, u32[]{:S(2)}, u32[]{:S(2)}) async-start(bf16[256,32,128]{2,0,1:T(8,128)(2,1)} %copy.45), calls=%async_computation.1 | async-start | bytes 4194304 | tf_op jit(solution)/shard_map/all_to_all | solution.py:51
  22.3 123.4 %all-gather.3.cloned.1.call-start = ((), (), s32[]{:S(2)}) async-start(), calls=%async_computation.4 | async-start | bytes 5591040 | tf_op jit(solution)/shard_map/all_gather | solution.py:23
  49.4 5.7 %copy-start.4 = (bf16[256,512]{1,0:T(8,128)(2,1)S(1)}, bf16[256,512]{1,0:T(8,128)(2,1)}, u32[]{:S(2)}) copy-start(bf16[256,512]{1,0:T(8,128)(2,1)} %param.8) | copy-start | bytes 786436
  55.9 9.4 %all-to-all-start.2 = ((bf16[256,32,16]{0,2,1:T(8,128)(2,1)}), bf16[256,32,16]{0,2,1:T(8,128)(2,1)S(1)}, u32[]{:S(2)}, u32[]{:S(2)}) async-start(bf16[256,32,16]{0,2,1:T(8,128)(2,1)} %bitcast.17), calls=%async_computation.2 | async-start | bytes 524288 | tf_op jit(solution)/shard_map/all_to_all | solution.py:49
  59.4 11.9 %collective-permute-start.1 = (bf16[64,8,16]{0,2,1:T(8,128)(2,1)S(1)}, bf16[64,8,16]{0,2,1:T(8,128)(2,1)S(1)}, u32[]{:S(2)}, u32[]{:S(2)}) collective-permute-start(bf16[64,8,16]{0,2,1:T(8,128)(2,1)S(1)} %slice.9), channel_id=1, source_target_pairs={{0,4},{4,8},{8,12},{1,5},{5,9},{9,13},{2,6},{6,10},{10,14},{3,7},{... | collective-permute-start | bytes 49160 | tf_op jit(solution)/shard_map/ppermute | solution.py:18
  67.0 10.3 %collective-permute-start = (bf16[64,8,128]{2,0,1:T(8,128)(2,1)S(1)}, bf16[64,8,128]{2,0,1:T(8,128)(2,1)S(1)}, u32[]{:S(2)}, u32[]{:S(2)}) collective-permute-start(bf16[64,8,128]{2,0,1:T(8,128)(2,1)S(1)} %slice.8), channel_id=1, source_target_pairs={{0,4},{4,8},{8,12},{1,5},{5,9},{9,13},{2,6},{6,10},{10,14},{3,7},{... | collective-permute-start | bytes 393224 | tf_op jit(solution)/shard_map/ppermute | solution.py:18
  153.2 4.6 %copy-start.1 = (bf16[1024,8,16]{0,2,1:T(8,128)(2,1)}, bf16[1024,8,16]{0,2,1:T(8,128)(2,1)S(1)}, u32[]{:S(2)}) copy-start(bf16[1024,8,16]{0,2,1:T(8,128)(2,1)S(1)} %get-tuple-element.497) | copy-start | bytes 786436 | tf_op jit(solution)/shard_map/while
  163.5 4.4 %slice-start = ((s8[4587520]{0:T(1024)(128)(4,1)}), s8[4194304]{0:T(1024)(128)(4,1)S(1)}, s32[]{:S(2)}) async-start(s8[4587520]{0:T(1024)(128)(4,1)} %bitcast.74), calls=%async_computation.5 | async-start | bytes 8388608 | tf_op jit(solution)/shard_map/while
  164.2 3.7 %slice-start.1 = ((s8[4587520]{0:T(1024)(128)(4,1)}), s8[393216]{0:T(1024)(128)(4,1)S(1)}, s32[]{:S(2)}) async-start(s8[4587520]{0:T(1024)(128)(4,1)} %bitcast.74), calls=%async_computation.6 | async-start | bytes 786432 | tf_op jit(solution)/shard_map/while
  167.9 2.3 copy-start
  167.9 2.3 copy-start.3
  185.1 3.6 %copy-start.2 = (bf16[1024,8,16]{0,2,1:T(8,128)(2,1)S(1)}, bf16[1024,8,16]{0,2,1:T(8,128)(2,1)}, u32[]{:S(2)}) copy-start(bf16[1024,8,16]{0,2,1:T(8,128)(2,1)} %copy-done.1) | copy-start | bytes 786436 | tf_op jit(solution)/shard_map/while
  188.7 4.6 %copy-start.1 = (bf16[1024,8,16]{0,2,1:T(8,128)(2,1)}, bf16[1024,8,16]{0,2,1:T(8,128)(2,1)S(1)}, u32[]{:S(2)}) copy-start(bf16[1024,8,16]{0,2,1:T(8,128)(2,1)S(1)} %get-tuple-element.497) | copy-start | bytes 786436 | tf_op jit(solution)/shard_map/while
  198.9 4.4 %slice-start = ((s8[4587520]{0:T(1024)(128)(4,1)}), s8[4194304]{0:T(1024)(128)(4,1)S(1)}, s32[]{:S(2)}) async-start(s8[4587520]{0:T(1024)(128)(4,1)} %bitcast.74), calls=%async_computation.5 | async-start | bytes 8388608 | tf_op jit(solution)/shard_map/while
  199.6 3.7 %slice-start.1 = ((s8[4587520]{0:T(1024)(128)(4,1)}), s8[393216]{0:T(1024)(128)(4,1)S(1)}, s32[]{:S(2)}) async-start(s8[4587520]{0:T(1024)(128)(4,1)} %bitcast.74), calls=%async_computation.6 | async-start | bytes 786432 | tf_op jit(solution)/shard_map/while
  203.4 2.4 copy-start
  203.4 2.4 copy-start.3
  220.6 3.6 %copy-start.2 = (bf16[1024,8,16]{0,2,1:T(8,128)(2,1)S(1)}, bf16[1024,8,16]{0,2,1:T(8,128)(2,1)}, u32[]{:S(2)}) copy-start(bf16[1024,8,16]{0,2,1:T(8,128)(2,1)} %copy-done.1) | copy-start | bytes 786436 | tf_op jit(solution)/shard_map/while
  227.0 5.5 %copy-start.5 = (f32[1024]{0:T(1024)S(1)}, f32[1024]{0:T(1024)}, u32[]{:S(2)}) copy-start(f32[1024]{0:T(1024)} %param.11) | copy-start | bytes 12292
Sparse Core Ops, SparseCore 0:
  55.2 90.4 all-gather.2
where the time goes:
time: 280 us; the launch traced here: 279 us
  waiting for transfers between devices  92.4 us (33%)
  matrix products  55.3 us (20%)
  local copies, waits for them, and re-layouts  39.3 us (14%)
  blocking collectives  28.8 us (10%)
  other arithmetic  28.4 us (10%)
  starting transfers between devices  19.7 us (7%)
  between operations  13.6 us (5%)
    all_gather x1, waiting for transfers between devices, entering(): everything = lax.all_gather(shard, axis)  65.2 us
    all_to_all x1, blocking collectives, per_device(): lax.all_to_all(mixed, 'head', split_axis=0, concat_axis=1, tiled=True)  28.8 us
    all_to_all x1, waiting for transfers between devices, per_device(): lax.all_to_all(value_tok, 'head', split_axis=1, concat_axis=0, tiled=True)  20.3 us
    sub x2, matrix products, block_step(): expo = jnp.where(valid, jnp.exp(window_scores - highest_score), 0.0)  16.7 us
    dot_general x2, matrix products, block_step(): jnp.einsum('hbc,chv->bhv', weights, value_window, preferred_element_type=...  13 us
    dot_general x2, matrix products, block_step(): jnp.einsum('hbc,chv->bhv', kernel, value_block, preferred_element_type=jn...  9.1 us
    ppermute x2, starting transfers between devices, shifted(): return lax.ppermute(shard, axis, pairs)  8.46 us
    dot_general x2, matrix products, block_step(): jnp.einsum('bhf,hfv->bhv', query_feat, state.astype(jnp.bfloat16), prefer...  7.45 us
  transfers between devices with their start and end apart: 6, of which 4 were waited for; matrix products, arithmetic and copies ran while one was open for 6% of the time, Pallas kernels for 0%

commit v1 on v0

--- a/solution.py
+++ b/solution.py
@@ -41,12 +41,21 @@
 
 
 def per_device(queries, keys, values, gain):
+
+    def process_area(join_dim, field_in, dimension_no):
+        return jnp.concatenate(
+            lax.all_to_all(
+                jnp.stack(jnp.split(field_in, lax.psum(1, "head"), axis=join_dim)), "head", 0, 0
+            ),
+            axis=dimension_no,
+        )
+
     local_tokens = queries.shape[0]
     query_tok = queries.reshape(local_tokens, HEADS, KD)
     key_tok = keys.reshape(local_tokens, HEADS, KD)
     value_tok = values.reshape(local_tokens, HEADS, VD)
     query_head, key_head, value_head = (
-        lax.all_to_all(query_tok, "head", split_axis=1, concat_axis=0, tiled=True),
+        process_area(1, query_tok, 0),
         lax.all_to_all(key_tok, "head", split_axis=1, concat_axis=0, tiled=True),
         lax.all_to_all(value_tok, "head", split_axis=1, concat_axis=0, tiled=True),
     )

time: 280 us -> 280 us (level)
  waiting for transfers between devices: 92.4 us -> 88.7 us
  other arithmetic: 28.4 us -> 32 us
    another operation x8 -> x9, other arithmetic: 5.83 us -> 7.56 us
  transfers between devices with their start and end apart: 6 -> 6, of which waited for: 4 -> 4; matrix products, arithmetic and copies ran while one was open for 6% -> 8% of each run, Pallas kernels for 0% -> 0%
where the time goes in v1:
time: 280 us; the launch traced here: 279 us
  waiting for transfers between devices  88.7 us (32%)
  matrix products  55.3 us (20%)
  local copies, waits for them, and re-layouts  39.8 us (14%)
  other arithmetic  32 us (11%)
  blocking collectives  28.4 us (10%)
  starting transfers between devices  19.7 us (7%)
  between operations  13.6 us (5%)
    all_gather x1, waiting for transfers between devices, entering(): everything = lax.all_gather(shard, axis)  65.9 us
    all_to_all x1, blocking collectives, per_device(): lax.all_to_all(mixed, 'head', split_axis=0, concat_axis=1, tiled=True)  28.4 us
    all_to_all x1, waiting for transfers between devices, per_device(): lax.all_to_all(value_tok, 'head', split_axis=1, concat_axis=0, tiled=True)  17.6 us
    sub x2, matrix products, block_step(): expo = jnp.where(valid, jnp.exp(window_scores - highest_score), 0.0)  16.7 us
    dot_general x2, matrix products, block_step(): jnp.einsum('hbc,chv->bhv', weights, value_window, preferred_element_type=...  13 us
    dot_general x2, matrix products, block_step(): jnp.einsum('hbc,chv->bhv', kernel, value_block, preferred_element_type=jn...  9.09 us
    ppermute x2, starting transfers between devices, shifted(): return lax.ppermute(shard, axis, pairs)  8.46 us
    dot_general x2, matrix products, block_step(): jnp.einsum('bhf,hfv->bhv', query_feat, state.astype(jnp.bfloat16), prefer...  7.46 us
  transfers between devices with their start and end apart: 6, of which 4 were waited for; matrix products, arithmetic and copies ran while one was open for 8% of the time, Pallas kernels for 0%

profile of v1, /device:TPU:0, one launch (start us, length us, event | category | flops | bytes accessed | tf_op | source)
XLA Modules:
  0.0 279.0 jit_solution(16212991702656598304)
XLA Ops:
  6.5 1.8 copy.46
  8.3 4.2 %all-to-all-start = ((bf16[256,32,16]{0,2,1:T(8,128)(2,1)}), bf16[256,32,16]{0,2,1:T(8,128)(2,1)S(1)}, u32[]{:S(2)}, u32[]{:S(2)}) async-start(bf16[256,32,16]{0,2,1:T(8,128)(2,1)} %bitcast.7), calls=%async_computation | async-start | bytes 524288 | tf_op jit(solution)/shard_map/all_to_all | solution.py:59
  12.5 3.3 %copy.48 = bf16[256,4096]{0,1:T(8,128)(2,1)S(1)} copy(bf16[256,4096]{1,0:T(8,128)(2,1)} %param.10) | data formatting | bytes 4194304 | tf_op args[2]
  15.8 2.9 %copy.49 = bf16[256,32,128]{2,0,1:T(8,128)(2,1)} copy(bf16[256,32,128]{0,2,1:T(8,128)(2,1)S(1)} %bitcast.85) | data formatting | bytes 4194304 | tf_op jit(solution)/shard_map/reshape | solution.py:56
  18.7 3.6 %all-to-all-start.1 = ((bf16[256,32,128]{2,0,1:T(8,128)(2,1)}), bf16[256,32,128]{2,0,1:T(8,128)(2,1)S(1)}, u32[]{:S(2)}, u32[]{:S(2)}) async-start(bf16[256,32,128]{2,0,1:T(8,128)(2,1)} %copy.49), calls=%async_computation.1 | async-start | bytes 4194304 | tf_op jit(solution)/shard_map/all_to_all | solution.py:60
  22.4 0.8 copy.68
  23.1 1.0 convert_element_type.48
  24.1 1.0 multiply_convert_fusion.3
  25.1 1.4 multiply_convert_fusion.2
  26.5 3.9 %pad_maximum_fusion = bf16[1024,8,273]{0,2,1:T(8,128)(2,1)} fusion(bf16[1024,8,256]{0,2,1:T(8,128)(2,1)S(1)} %bitcast.81, bf16[1024,8,16]{0,2,1:T(8,128)(2,1)S(1)} %multiply_convert_fusion.3, bf16[273]{0:T(512)(128)(2,1)S(1)} %pad.11.clone), kind=kLoop, calls=%fused_computation.66 | loop fusion | flops 13418496 | bytes 8929826 | tf_op jit(solution)/shard_map/concatenate | solution.py:40
  30.4 17.6 %all-to-all-done.1 = bf16[256,32,128]{2,0,1:T(8,128)(2,1)S(1)} async-done(((bf16[256,32,128]{2,0,1:T(8,128)(2,1)}), bf16[256,32,128]{2,0,1:T(8,128)(2,1)S(1)}, u32[]{:S(2)}, u32[]{:S(2)}) %all-to-all-start.1) | async-done | bytes 2097184 | tf_op jit(solution)/shard_map/all_to_all | solution.py:60
  48.0 1.5 copy.51
  49.4 4.4 %fusion.77 = f32[8,273,128]{2,1,0:T(8,128)S(1)} fusion(bf16[1024,8,273]{0,2,1:T(8,128)(2,1)} %pad_maximum_fusion, bf16[1024,8,128]{2,0,1:T(8,128)(2,1)} %bitcast.15), kind=kOutput, calls=%fused_computation.82 | convolution fusion | flops 572522496 | bytes 7688192 | tf_op jit(solution)/shard_map/bhf,bhv->hfv/dot_general | solution.py:73
  53.8 1.3 copy.52
  55.3 0.7 pad_maximum_fusion.3
  56.0 3.4 %all-to-all-start.2 = ((bf16[4,256,8,16]{1,3,2,0:T(8,128)(2,1)}), bf16[4,256,8,16]{1,3,2,0:T(8,128)(2,1)S(1)}, u32[]{:S(2)}, u32[]{:S(2)}) async-start(bf16[4,256,8,16]{1,3,2,0:T(8,128)(2,1)} %pad_maximum_fusion.3), calls=%async_computation.2 | async-start | bytes 524288 | tf_op jit(solution)/shard_map/all_to_all | solution.py:47
  59.4 0.8 slice.9
  60.3 4.1 %collective-permute-start.1 = (bf16[64,8,16]{0,2,1:T(8,128)(2,1)S(1)}, bf16[64,8,16]{0,2,1:T(8,128)(2,1)S(1)}, u32[]{:S(2)}, u32[]{:S(2)}) collective-permute-start(bf16[64,8,16]{0,2,1:T(8,128)(2,1)S(1)} %slice.9), channel_id=1, source_target_pairs={{0,4},{4,8},{8,12},{1,5},{5,9},{9,13},{2,6},{6,10},{10,14},{3,7},{... | collective-permute-start | bytes 49160 | tf_op jit(solution)/shard_map/ppermute | solution.py:18
  64.4 1.0 all-to-all-done.2
  65.4 0.8 copy.69
  66.2 0.9 slice.8
  67.1 4.3 %collective-permute-start = (bf16[64,8,128]{2,0,1:T(8,128)(2,1)S(1)}, bf16[64,8,128]{2,0,1:T(8,128)(2,1)S(1)}, u32[]{:S(2)}, u32[]{:S(2)}) collective-permute-start(bf16[64,8,128]{2,0,1:T(8,128)(2,1)S(1)} %slice.8), channel_id=1, source_target_pairs={{0,4},{4,8},{8,12},{1,5},{5,9},{9,13},{2,6},{6,10},{10,14},{3,7},{... | collective-permute-start | bytes 393224 | tf_op jit(solution)/shard_map/ppermute | solution.py:18
  71.4 1.8 pad_maximum_fusion.2
  73.3 4.2 %collective-permute-done = bf16[64,8,128]{2,0,1:T(8,128)(2,1)S(1)} collective-permute-done((bf16[64,8,128]{2,0,1:T(8,128)(2,1)S(1)}, bf16[64,8,128]{2,0,1:T(8,128)(2,1)S(1)}, u32[]{:S(2)}, u32[]{:S(2)}) %collective-permute-start) | collective-permute-done | bytes 131104 | tf_op jit(solution)/shard_map/ppermute | solution.py:18
  77.4 3.1 %pad_maximum_fusion.1 = bf16[1088,8,128]{2,0,1:T(8,128)(2,1)} fusion(bf16[1024,8,128]{2,0,1:T(8,128)(2,1)} %bitcast.15, bf16[64,8,128]{2,0,1:T(8,128)(2,1)S(1)} %collective-permute-done), kind=kLoop, calls=%fused_computation.72 | loop fusion | flops 4456448 | bytes 4456448 | tf_op jit(solution)/shard_map/concatenate | solution.py:70
  80.6 65.9 %all-gather.3.cloned.1.call-done = f32[32,273,128]{2,0,1:T(8,128)} async-done(((f32[8,273,128]{2,0,1:T(8,128)}), f32[32,273,128]{2,0,1:T(8,128)}) %all-gather.3.cloned.1.call-update) | async-done | bytes 4472848 | tf_op jit(solution)/shard_map/all_gather | solution.py:23
  146.4 7.5 %while.32 = (s32[]{:T(128)}, f32[8,273,128]{2,1,0:T(8,128)S(1)}, s32[]{:T(128)}, f32[4,8,273,128]{3,1,0,2:T(8,128)}, s32[]{:T(128)}, /*index=5*/s32[]{:T(128)}) while((s32[]{:T(128)}, f32[8,273,128]{2,1,0:T(8,128)S(1)}, s32[]{:T(128)}, f32[4,8,273,128]{3,1,0,2:T(8,128)}, s32[]{:T(128)}, /*index=5*/s32[]{:T(128)}) %tuple.72), condition=%wide.region_1.2_spmd.clone, body=%wide.region_0.1_spmd.clone.sunk | while | flops 838660 | bytes 5591141 | solution.py:31
  146.4 1.3 constant_dynamic-slice_fusion.2
  148.3 1.3 constant_dynamic-slice_fusion.2
  150.2 1.3 constant_dynamic-slice_fusion.2
  152.1 1.3 constant_dynamic-slice_fusion.2
  154.0 70.8 %while.31 = (s32[]{:T(128)}, f32[8,273,128]{2,1,0:T(8,128)S(1)}, f32[2,512,8,128]{1,3,2,0:T(8,128)}, f32[2,512,8,128]{3,2,1,0:T(8,128)}, s32[2]{0:T(128)S(1)}, /...) while((s32[]{:T(128)}, f32[8,273,128]{2,1,0:T(8,128)S(1)}, ...), condition=%wide.region_5.6_spmd, body=%wide.region_2.5_spmd.sunk | while | flops 1977677568 | bytes 68214352 | solution.py:129
  154.0 0.6 dynamic_slice.126
  155.2 1.6 multiply_convert_fusion.7
  156.8 0.9 dynamic-slice_convert_fusion.2
  157.7 0.8 iota_compare_fusion.3
  158.5 1.1 fusion.113
  159.6 4.5 %fusion.111 = f32[8,128,512]{2,1,0:T(8,128)S(1)} fusion(pred[512,512]{1,0:T(8,128)(4,1)} %iota_compare_fusion.3, bf16[1024,8,128]{2,0,1:T(8,128)(2,1)} %get-tuple-element.499, s32[]{:T(128)S(6)} %select_n.84, bf16[1024,8,16]{0,2,1:T(8,128)(2,1)} %get-tuple-element.501, bf16[1024,8,16]{0,2,1:T(8,128)(2,1)} %get-tuple-element.500), kind=kOutput, calls=%fused_computation.12.clone.1 | convolution fusion | flops 618659840 | bytes 3671552 | tf_op jit(solution)/shard_map/while/body/eval_jaxpr/hbc,chv->bhv/dot_general | solution.py:99
  164.2 0.7 multiply_convert_fusion.6
  164.9 3.7 %bitcast_dynamic-update-slice_fusion.2 = f32[2,512,8,128]{1,3,2,0:T(8,128)} fusion(f32[2,512,8,128]{1,3,2,0:T(8,128)} %get-tuple-element.476, s32[]{:T(128)S(6)} %copy.89, f32[8,128,512]{2,1,0:T(8,128)S(1)} %fusion.111, bf16[512,8,256]{0,2,1:T(8,128)(2,1)S(1)} %bitcast.78, bf16[512,8,16]{0,2,1:T(8,128)(2,1)} %multiply_convert_fusion.7, ...), kind=kOutput, calls=%fused_computation.22.clone.1 | convolution fusion | flops 293774336 | bytes 7541286 | tf_op jit(solution)/shard_map/while/body/eval_jaxpr/bhf,hfv->bhv/dot_general | solution.py:101
  168.6 2.3 fusion.110
  170.9 8.3 %fusion.114 = (f32[8,512]{1,0:T(8,128)S(1)}, f32[8,512,576]{1,2,0:T(8,128)}) fusion(pred[512,576]{0,1:T(8,128)(4,1)S(1)} %copy-done, bf16[1088,8,16]{0,2,1:T(8,128)(2,1)S(1)} %copy-done.1, s32[]{:T(128)S(6)} %select_n.85, bf16[1024,8,16]{0,2,1:T(8,128)(2,1)} %get-tuple-element.500, s32[]{:T(128)S(6)} %select_n.84), kind=kOutput, calls=%fused_computation.81.clone.1 | convolution fusion | flops 165151296 | bytes 10635264 | tf_op jit(solution)/shard_map/while/body/eval_jaxpr/sub | solution.py:122
  179.3 6.5 %fusion.115 = f32[1,512,8,128]{1,3,2,0:T(8,128)} fusion(f32[8,512,576]{1,2,0:T(8,128)} %get-tuple-element.431, f32[8,512]{1,0:T(8,128)S(1)} %get-tuple-element.432, bf16[1088,8,128]{2,0,1:T(8,128)(2,1)} %get-tuple-element.502, s32[]{:T(128)S(6)} %select_n.85), kind=kOutput, calls=%fused_computation.24.clone.1 | convolution fusion | flops 608698368 | bytes 12730372 | tf_op jit(solution)/shard_map/while/body/eval_jaxpr/hbc,chv->bhv/dot_general | solution.py:124
  185.8 2.1 copy.75
  187.9 1.5 constant_dynamic-update-slice_fusion.2
  189.3 0.6 dynamic_slice.126
  190.6 1.6 multiply_convert_fusion.7
  192.1 0.9 dynamic-slice_convert_fusion.2
  193.1 0.8 iota_compare_fusion.3
  193.9 1.1 fusion.113
  195.0 4.5 %fusion.111 = f32[8,128,512]{2,1,0:T(8,128)S(1)} fusion(pred[512,512]{1,0:T(8,128)(4,1)} %iota_compare_fusion.3, bf16[1024,8,128]{2,0,1:T(8,128)(2,1)} %get-tuple-element.499, s32[]{:T(128)S(6)} %select_n.84, bf16[1024,8,16]{0,2,1:T(8,128)(2,1)} %get-tuple-element.501, bf16[1024,8,16]{0,2,1:T(8,128)(2,1)} %get-tuple-element.500), kind=kOutput, calls=%fused_computation.12.clone.1 | convolution fusion | flops 618659840 | bytes 3671552 | tf_op jit(solution)/shard_map/while/body/eval_jaxpr/hbc,chv->bhv/dot_general | solution.py:99
  199.5 0.7 multiply_convert_fusion.6
  200.2 3.7 %bitcast_dynamic-update-slice_fusion.2 = f32[2,512,8,128]{1,3,2,0:T(8,128)} fusion(f32[2,512,8,128]{1,3,2,0:T(8,128)} %get-tuple-element.476, s32[]{:T(128)S(6)} %copy.89, f32[8,128,512]{2,1,0:T(8,128)S(1)} %fusion.111, bf16[512,8,256]{0,2,1:T(8,128)(2,1)S(1)} %bitcast.78, bf16[512,8,16]{0,2,1:T(8,128)(2,1)} %multiply_convert_fusion.7, ...), kind=kOutput, calls=%fused_computation.22.clone.1 | convolution fusion | flops 293774336 | bytes 7541286 | tf_op jit(solution)/shard_map/while/body/eval_jaxpr/bhf,hfv->bhv/dot_general | solution.py:101
  203.9 2.3 fusion.110
  206.3 8.3 %fusion.114 = (f32[8,512]{1,0:T(8,128)S(1)}, f32[8,512,576]{1,2,0:T(8,128)}) fusion(pred[512,576]{0,1:T(8,128)(4,1)S(1)} %copy-done, bf16[1088,8,16]{0,2,1:T(8,128)(2,1)S(1)} %copy-done.1, s32[]{:T(128)S(6)} %select_n.85, bf16[1024,8,16]{0,2,1:T(8,128)(2,1)} %get-tuple-element.500, s32[]{:T(128)S(6)} %select_n.84), kind=kOutput, calls=%fused_computation.81.clone.1 | convolution fusion | flops 165151296 | bytes 10635264 | tf_op jit(solution)/shard_map/while/body/eval_jaxpr/sub | solution.py:122
  214.7 6.5 %fusion.115 = f32[1,512,8,128]{1,3,2,0:T(8,128)} fusion(f32[8,512,576]{1,2,0:T(8,128)} %get-tuple-element.431, f32[8,512]{1,0:T(8,128)S(1)} %get-tuple-element.432, bf16[1088,8,128]{2,0,1:T(8,128)(2,1)} %get-tuple-element.502, s32[]{:T(128)S(6)} %select_n.85), kind=kOutput, calls=%fused_computation.24.clone.1 | convolution fusion | flops 608698368 | bytes 12730372 | tf_op jit(solution)/shard_map/while/body/eval_jaxpr/hbc,chv->bhv/dot_general | solution.py:124
  221.2 2.1 copy.75
  223.3 1.5 constant_dynamic-update-slice_fusion.2
  224.8 2.8 multiply_reduce_fusion
  227.5 5.3 %copy.56 = f32[2,512,8,128]{3,2,1,0:T(8,128)} copy(f32[2,512,8,128]{1,3,2,0:T(8,128)} %get-tuple-element.272) | data formatting | bytes 8388608 | tf_op jit(solution)/shard_map/while | solution.py:129
  233.0 4.1 %fusion.66 = bf16[1024,8,128]{2,1,0:T(8,128)(2,1)S(1)} fusion(f32[2,512,8,128]{3,2,1,0:T(8,128)} %get-tuple-element.273, f32[2,512,8,128]{3,2,1,0:T(8,128)} %copy.56, f32[8,128]{1,0:T(8,128)S(1)} %bitcast.91, f32[1024,8]{1,0:T(8,128)S(1)} %copy.57), kind=kLoop, calls=%fused_computation.68 | loop fusion | flops 4194304 | bytes 10522624 | tf_op jit(solution)/shard_map/convert_element_type | solution.py:134
  237.1 28.4 %all_to_all.56 = bf16[1024,8,128]{2,1,0:T(8,128)(2,1)S(1)} all-to-all(bf16[1024,8,128]{2,1,0:T(8,128)(2,1)S(1)} %fusion.66), channel_id=1, replica_groups=mesh['groups'=2,'ctx'=4,'head'=4] {'head'}, dimensions={0} | all-to-all | bytes 4194304 | tf_op jit(solution)/shard_map/all_to_all | solution.py:135
  265.6 2.6 copy.59
  268.1 4.1 %copy.60 = bf16[256,4096]{1,0:T(8,128)(2,1)} copy(bf16[256,4096]{0,1:T(8,128)(2,1)} %bitcast.84) | data formatting | bytes 4194304 | tf_op jit(solution)/shard_map/reshape | solution.py:136
  (47 shorter events, 2.7 us)
Async XLA Ops:
  8.3 10.3 %all-to-all-start = ((bf16[256,32,16]{0,2,1:T(8,128)(2,1)}), bf16[256,32,16]{0,2,1:T(8,128)(2,1)S(1)}, u32[]{:S(2)}, u32[]{:S(2)}) async-start(bf16[256,32,16]{0,2,1:T(8,128)(2,1)} %bitcast.7), calls=%async_computation | async-start | bytes 524288 | tf_op jit(solution)/shard_map/all_to_all | solution.py:59
  18.7 29.3 %all-to-all-start.1 = ((bf16[256,32,128]{2,0,1:T(8,128)(2,1)}), bf16[256,32,128]{2,0,1:T(8,128)(2,1)S(1)}, u32[]{:S(2)}, u32[]{:S(2)}) async-start(bf16[256,32,128]{2,0,1:T(8,128)(2,1)} %copy.49), calls=%async_computation.1 | async-start | bytes 4194304 | tf_op jit(solution)/shard_map/all_to_all | solution.py:60
  22.3 124.1 %all-gather.3.cloned.1.call-start = ((), (), s32[]{:S(2)}) async-start(), calls=%async_computation.4 | async-start | bytes 5591040 | tf_op jit(solution)/shard_map/all_gather | solution.py:23
  49.4 5.7 %copy-start.2 = (bf16[256,512]{1,0:T(8,128)(2,1)S(1)}, bf16[256,512]{1,0:T(8,128)(2,1)}, u32[]{:S(2)}) copy-start(bf16[256,512]{1,0:T(8,128)(2,1)} %param.8) | copy-start | bytes 786436
  56.0 9.4 %all-to-all-start.2 = ((bf16[4,256,8,16]{1,3,2,0:T(8,128)(2,1)}), bf16[4,256,8,16]{1,3,2,0:T(8,128)(2,1)S(1)}, u32[]{:S(2)}, u32[]{:S(2)}) async-start(bf16[4,256,8,16]{1,3,2,0:T(8,128)(2,1)} %pad_maximum_fusion.3), calls=%async_computation.2 | async-start | bytes 524288 | tf_op jit(solution)/shard_map/all_to_all | solution.py:47
  60.3 11.2 %collective-permute-start.1 = (bf16[64,8,16]{0,2,1:T(8,128)(2,1)S(1)}, bf16[64,8,16]{0,2,1:T(8,128)(2,1)S(1)}, u32[]{:S(2)}, u32[]{:S(2)}) collective-permute-start(bf16[64,8,16]{0,2,1:T(8,128)(2,1)S(1)} %slice.9), channel_id=1, source_target_pairs={{0,4},{4,8},{8,12},{1,5},{5,9},{9,13},{2,6},{6,10},{10,14},{3,7},{... | collective-permute-start | bytes 49160 | tf_op jit(solution)/shard_map/ppermute | solution.py:18
  67.1 10.3 %collective-permute-start = (bf16[64,8,128]{2,0,1:T(8,128)(2,1)S(1)}, bf16[64,8,128]{2,0,1:T(8,128)(2,1)S(1)}, u32[]{:S(2)}, u32[]{:S(2)}) collective-permute-start(bf16[64,8,128]{2,0,1:T(8,128)(2,1)S(1)} %slice.8), channel_id=1, source_target_pairs={{0,4},{4,8},{8,12},{1,5},{5,9},{9,13},{2,6},{6,10},{10,14},{3,7},{... | collective-permute-start | bytes 393224 | tf_op jit(solution)/shard_map/ppermute | solution.py:18
  164.2 4.4 %slice-start = ((s8[4587520]{0:T(1024)(128)(4,1)}), s8[4194304]{0:T(1024)(128)(4,1)S(1)}, s32[]{:S(2)}) async-start(s8[4587520]{0:T(1024)(128)(4,1)} %bitcast.79), calls=%async_computation.5 | async-start | bytes 8388608 | tf_op jit(solution)/shard_map/while
  164.8 3.7 %slice-start.1 = ((s8[4587520]{0:T(1024)(128)(4,1)}), s8[393216]{0:T(1024)(128)(4,1)S(1)}, s32[]{:S(2)}) async-start(s8[4587520]{0:T(1024)(128)(4,1)} %bitcast.79), calls=%async_computation.6 | async-start | bytes 786432 | tf_op jit(solution)/shard_map/while
  168.6 2.3 copy-start
  168.6 2.3 copy-start.1
  199.5 4.4 %slice-start = ((s8[4587520]{0:T(1024)(128)(4,1)}), s8[4194304]{0:T(1024)(128)(4,1)S(1)}, s32[]{:S(2)}) async-start(s8[4587520]{0:T(1024)(128)(4,1)} %bitcast.79), calls=%async_computation.5 | async-start | bytes 8388608 | tf_op jit(solution)/shard_map/while
  200.2 3.7 %slice-start.1 = ((s8[4587520]{0:T(1024)(128)(4,1)}), s8[393216]{0:T(1024)(128)(4,1)S(1)}, s32[]{:S(2)}) async-start(s8[4587520]{0:T(1024)(128)(4,1)} %bitcast.79), calls=%async_computation.6 | async-start | bytes 786432 | tf_op jit(solution)/shard_map/while
  203.9 2.4 copy-start
  203.9 2.4 copy-start.1
  227.5 5.5 %copy-start.3 = (f32[1024]{0:T(1024)S(1)}, f32[1024]{0:T(1024)}, u32[]{:S(2)}) copy-start(f32[1024]{0:T(1024)} %param.11) | copy-start | bytes 12292
Sparse Core Ops, SparseCore 0:
  55.2 91.1 all-gather.2
